TPU v7x, 512 devices: a whole 4x4x16 slice. The times are simulated.
512 devices in a mesh: dp: 8 (over z_hi, core), dom: 64 (over x, z_lo, y).
Axes of the slice: x: 4, y: 4, z: 16 (z_hi: 4, z_lo: 4; z = z_hi * 4 + z_lo), core: 2. Of those that a mesh axis runs over, the one named last changes fastest.
Arguments:
- density: bfloat16 [8, 64, 512, 256], P('dp', None, 'dom'), may hold values from -6 to 6
- upstream: bfloat16 [8, 64, 512, 256], P('dp', None, 'dom'), may hold values from -6 to 6
- spectral_weight: float32 [2048, 64], P(('dp', 'dom')), may hold values from -0.5 to 0.5
- moment_one: float32 [2048, 64], P(('dp', 'dom')), may hold values from -128 to 128
- moment_two: float32 [2048, 64], P(('dp', 'dom')), may hold values from 256 to 4096
- skip_weight: bfloat16 [64, 64], replicated, may hold values from -0.75 to 0.75
- skip_bias: float32 [64], replicated, may hold values from -3 to 3
- mode_counts: int32 [8], replicated, may hold values from 8 to 16, as said below
Outputs:
- input_grad: bfloat16 [8, 64, 512, 256], P('dp', None, 'dom')
- new_weight: float32 [2048, 64], P(('dp', 'dom'))
- new_moment_one: float32 [2048, 64], P(('dp', 'dom'))
- new_moment_two: float32 [2048, 64], P(('dp', 'dom'))
Inputs may be any that keep to these rules, and one draw needn't show every extreme that they name: `mode_counts`: some entry equals 16.
All inputs are finite; a program needn't handle non-finite values.
Results may differ from a plain program's by a relative error of at most 0.0053.
Values may be sent and summed in bfloat16 or wider, within the bound.
No kernel may reach another device: no remote copies, remote signals or barrier semaphores. Data moves between devices by JAX's collectives and lax.ppermute only.
A program may use at most 64 MiB of HBM per device.

v0:
```python
import math
import jax
import jax.numpy as jnp
from jax import lax
from jax.sharding import PartitionSpec as P

MODES = 16
STEP = 10
learn_rate = 0.01
beta_first = 0.9
beta_second = 0.95
decay_rate = 0.1
epsilon = 1e-08


def joined_along(tiles, dim):
    dims = list(tiles.shape[1:])
    dims[dim] *= tiles.shape[0]
    return jnp.moveaxis(tiles, 0, dim).reshape(dims)


def copy_for_each(shard, axis):
    copies = jnp.broadcast_to(shard, (lax.axis_size(axis), *shard.shape))
    return lax.all_to_all(copies, axis, split_axis=0, concat_axis=0, tiled=True)


def collect(shard, axis, dim):
    return joined_along(copy_for_each(shard, axis), dim)


def in_one_piece(arrays, axis, split_dim, concat_dim, along):
    both = jnp.concatenate(arrays, axis=along)
    result, at, done = (
        lax.all_to_all(both, axis, split_axis=split_dim, concat_axis=concat_dim, tiled=True),
        0,
        [],
    )
    for a in arrays:
        done.append(lax.slice_in_dim(result, at, at + a.shape[along], axis=along))
        at += a.shape[along]
    return tuple(done)


def split_up(shard, dim, length):
    dims = shard.shape
    tiles = shard.reshape(*dims[:dim], length, dims[dim] // length, *dims[dim + 1 :])
    return jnp.moveaxis(tiles, dim, 0)


def sum_at_owner(shard, axis, dim):
    tiles = split_up(shard, dim, lax.axis_size(axis))
    arrived = lax.all_to_all(tiles, axis, split_axis=0, concat_axis=0, tiled=True)
    return arrived.astype(jnp.float32).sum(axis=0)


def summed_on_arrival(shard, axis, dim):
    length = lax.axis_size(axis)
    tiles = lax.all_to_all(split_up(shard, dim, length), axis, 0, 0, tiled=True)
    return jnp.sum(tiles, axis=0)


def axis_parts(count_xdim):
    freq_list = jnp.arange(MODES, dtype=jnp.int32)
    cell_list = jnp.arange(count_xdim, dtype=jnp.int32)
    phases = (
        jnp.mod(freq_list[:, None] * cell_list[None, :], count_xdim).astype(jnp.float32)
        / count_xdim
    )
    angles = 2.0 * math.pi * phases
    scaling = 1.0 / math.sqrt(count_xdim)
    return (
        (jnp.cos(angles) * scaling).astype(jnp.bfloat16),
        (jnp.sin(angles) * scaling).astype(jnp.bfloat16),
    )


def doubling_table():
    return jnp.where(jnp.arange(MODES, dtype=jnp.int32) > 0, 2.0, 1.0).astype(jnp.float32)


def gelu_slope(values):
    cumulative = 0.5 * (1.0 + lax.erf(values * 0.7071067811865476))
    bell_curve = jnp.exp(-0.5 * values * values) * 0.3989422804014327
    return cumulative + values * bell_curve


def forward_parts(field, cosines, sines):
    real_part = jnp.einsum("scxl,fx->slcf", field, cosines, preferred_element_type=jnp.float32)
    imag_part = -jnp.einsum("scxl,fx->slcf", field, sines, preferred_element_type=jnp.float32)
    return (real_part, imag_part)


def inverse_cells(values_real, values_imag, cosines, sines):
    first = jnp.einsum("slcf,fx->scxl", values_real, cosines, preferred_element_type=jnp.float32)
    second = jnp.einsum("slcf,fx->scxl", values_imag, sines, preferred_element_type=jnp.float32)
    return (first - second).astype(jnp.bfloat16)


def on_device(
    density, upstream, spectral_weight, moment_one, moment_two, skip_weight, skip_bias, mode_counts
):
    samples, channels, slab_rows, line_count = density.shape
    count_xdim = slab_rows * lax.axis_size("dom")
    cosines, sines = axis_parts(count_xdim)
    doubling = doubling_table()
    doubling_low = doubling.astype(jnp.bfloat16)
    counts_here = lax.dynamic_slice_in_dim(mode_counts, lax.axis_index("dp") * samples, samples, 0)
    keep_modes = (jnp.arange(MODES, dtype=jnp.int32)[None, :] < counts_here[:, None]).astype(
        jnp.float32
    )
    keep_wide = keep_modes[:, None, None, :]
    weight_short = spectral_weight.astype(jnp.bfloat16)
    group_low = collect(weight_short, "dom", 0)
    weight_low = lax.all_gather(group_low, "dp", axis=0, tiled=True)
    weight_low = weight_low.reshape(2, MODES, channels, channels)
    weight_real = weight_low[0]
    weight_imag = weight_low[1]
    density_lines, upstream_lines = in_one_piece((density, upstream), "dom", 3, 2, 0)
    real_part, imag_part = forward_parts(density_lines, cosines, sines)
    spec_real = real_part.astype(jnp.bfloat16)
    spec_imag = imag_part.astype(jnp.bfloat16)
    form = "slcf,fco->slof"
    mixed_real = jnp.einsum(
        form, spec_real, weight_real, preferred_element_type=jnp.float32
    ) - jnp.einsum(form, spec_imag, weight_imag, preferred_element_type=jnp.float32)
    mixed_imag = jnp.einsum(
        form, spec_imag, weight_real, preferred_element_type=jnp.float32
    ) + jnp.einsum(form, spec_real, weight_imag, preferred_element_type=jnp.float32)
    mixed_real = (mixed_real * keep_wide).astype(jnp.bfloat16) * doubling_low
    mixed_imag = (mixed_imag * keep_wide).astype(jnp.bfloat16) * doubling_low
    back_lines = inverse_cells(mixed_real, mixed_imag, cosines, sines)
    back_rows = lax.optimization_barrier(back_lines)
    skip_part = jnp.einsum(
        "oc,scxl->soxl", skip_weight, density_lines, preferred_element_type=jnp.float32
    )
    before = back_rows.astype(jnp.float32) + skip_part + skip_bias[None, :, None, None]
    gate_lines = (upstream_lines.astype(jnp.float32) * gelu_slope(before)).astype(jnp.bfloat16)
    grad_real, grad_imag = forward_parts(gate_lines, cosines, sines)
    scale = keep_wide * doubling
    grad_real = (grad_real * scale).astype(jnp.bfloat16)
    grad_imag = (grad_imag * scale).astype(jnp.bfloat16)
    outer = "slof,slcf->fco"
    part_real = jnp.einsum(
        outer, grad_real, spec_real, preferred_element_type=jnp.float32
    ) + jnp.einsum(outer, grad_imag, spec_imag, preferred_element_type=jnp.float32)
    part_imag = jnp.einsum(
        outer, grad_imag, spec_real, preferred_element_type=jnp.float32
    ) - jnp.einsum(outer, grad_real, spec_imag, preferred_element_type=jnp.float32)
    grad_local = jnp.stack([part_real, part_imag], 0).reshape(2 * MODES * channels, channels)
    group_grad = sum_at_owner(grad_local.astype(jnp.bfloat16), "dp", 0)
    weight_grad = summed_on_arrival(group_grad, "dom", 0)
    inner = "fco,slof->slcf"
    input_real = jnp.einsum(
        inner, weight_real, grad_real, preferred_element_type=jnp.float32
    ) + jnp.einsum(inner, weight_imag, grad_imag, preferred_element_type=jnp.float32)
    input_imag = jnp.einsum(
        inner, weight_real, grad_imag, preferred_element_type=jnp.float32
    ) - jnp.einsum(inner, weight_imag, grad_real, preferred_element_type=jnp.float32)
    input_lines = inverse_cells(
        input_real.astype(jnp.bfloat16), input_imag.astype(jnp.bfloat16), cosines, sines
    )
    input_rows = lax.optimization_barrier(input_lines)
    skip_back = jnp.einsum(
        "oc,soxl->scxl", skip_weight, gate_lines, preferred_element_type=jnp.float32
    )
    grad_lines = (input_rows.astype(jnp.float32) + skip_back).astype(jnp.bfloat16)
    input_grad = lax.all_to_all(grad_lines, "dom", split_axis=2, concat_axis=3, tiled=True)
    new_moment_one = beta_first * moment_one + (1.0 - beta_first) * weight_grad
    new_moment_two = beta_second * moment_two + (1.0 - beta_second) * weight_grad * weight_grad
    first_hat = new_moment_one / (1.0 - beta_first**STEP)
    second_hat = new_moment_two / (1.0 - beta_second**STEP)
    new_weight = spectral_weight - learn_rate * (
        first_hat / (jnp.sqrt(second_hat) + epsilon) + decay_rate * spectral_weight
    )
    return (input_grad, new_weight, new_moment_one, new_moment_two)


def solution(mesh):
    placed = (
        P("dp", None, "dom", None),
        P("dp", None, "dom", None),
        P(("dp", "dom"), None),
        P(("dp", "dom"), None),
        P(("dp", "dom"), None),
        P(),
        P(),
        P(),
    )
    return jax.shard_map(
        on_device,
        mesh=mesh,
        in_specs=placed,
        out_specs=(
            P("dp", None, "dom", None),
            P(("dp", "dom"), None),
            P(("dp", "dom"), None),
            P(("dp", "dom"), None),
        ),
        check_vma=False,
    )
```

profile of v0, /device:TPU:2, one launch (start us, length us, event | category | flops | bytes accessed | tf_op | source)
XLA Modules:
  0.0 135.0 jit_solution(11157942799677007264)
XLA Ops:
  0.6 0.7 convert_element_type.173
  1.4 0.7 reshape.173
  2.1 12.1 %all-to-all-start.1 = ((bf16[64,2,128]{2,1,0:T(2,128)(2,1)}), bf16[64,2,128]{2,1,0:T(2,128)(2,1)S(1)}, u32[]{:S(2)}, u32[]{:S(2)}) async-start(bf16[64,2,128]{2,1,0:T(2,128)(2,1)} %reshape.173), calls=%async_computation.1 | async-start | bytes 65536 | tf_op jit(solution)/shard_map/all_to_all | solution.py:24
  14.2 1.5 %copy.138 = bf16[1,64,8,256]{1,2,0,3:T(8,128)(2,1)S(1)} copy(bf16[1,64,8,256]{3,2,1,0:T(8,128)(2,1)} %param.9) | data formatting | bytes 524288 | tf_op args[1]
  15.7 0.4 copy.137
  16.1 0.2 fusion.144
  16.3 1.5 %reshape.171 = bf16[64,2,2048]{2,1,0:T(2,128)(2,1)} reshape(bf16[256,2,8,64]{3,2,1,0:T(8,128)(2,1)S(1)} %fusion.144) | data formatting | bytes 1048576
  17.9 5.4 %all-to-all-done.1 = bf16[64,2,128]{2,1,0:T(2,128)(2,1)S(1)} async-done(((bf16[64,2,128]{2,1,0:T(2,128)(2,1)}), bf16[64,2,128]{2,1,0:T(2,128)(2,1)S(1)}, u32[]{:S(2)}, u32[]{:S(2)}) %all-to-all-start.1) | async-done | bytes 32800 | tf_op jit(solution)/shard_map/all_to_all | solution.py:24
  23.2 5.5 %all-to-all-start = ((bf16[64,2,2048]{2,1,0:T(2,128)(2,1)}), bf16[64,2,2048]{2,1,0:T(2,128)(2,1)S(1)}, u32[]{:S(2)}, u32[]{:S(2)}) async-start(bf16[64,2,2048]{2,1,0:T(2,128)(2,1)} %reshape.171), calls=%async_computation | async-start | bytes 1048576 | tf_op jit(solution)/shard_map/all_to_all | solution.py:34
  28.8 0.6 copy-done.5
  29.4 0.6 dynamic_slice.3
  30.0 0.6 compare_convert_fusion
  30.7 0.7 compare_select_fusion.1
  31.4 25.7 %all_gather.3 = bf16[2048,64]{1,0:T(8,128)(2,1)S(1)} all-gather(bf16[256,64]{1,0:T(8,128)(2,1)S(1)} %bitcast.194), channel_id=1, replica_groups=mesh['dp'=8,'dom'=64] {'dp'}, dimensions={0}, use_global_device_ids=true | all-gather | bytes 294912 | tf_op jit(solution)/shard_map/all_gather | solution.py:114
  57.2 0.7 reshape.172
  58.1 0.3 fusion.34
  58.4 0.3 fusion.35
  58.7 0.3 copy.151
  59.6 0.3 fusion.67
  60.2 0.3 fusion.11
  60.5 0.3 copy-done.6
  60.8 0.5 fusion.47
  61.3 0.3 fusion.29
  61.5 0.3 fusion.28
  62.0 0.3 fusion.84
  62.4 0.3 fusion.77
  62.9 0.3 fusion.8
  63.2 0.3 fusion.9
  63.6 0.9 copy.170
  64.5 6.4 %all-to-all-start.3 = ((bf16[8,256,64]{1,2,0:T(8,128)(2,1)}), bf16[8,256,64]{1,2,0:T(8,128)(2,1)S(1)}, u32[]{:S(2)}, u32[]{:S(2)}) async-start(bf16[8,256,64]{1,2,0:T(8,128)(2,1)} %copy.170), calls=%async_computation.3 | async-start | bytes 524288 | tf_op jit(solution)/shard_map/all_to_all | solution.py:52
  71.2 0.3 fusion.26
  71.4 0.4 fusion.64
  71.8 0.3 fusion.10
  72.1 0.3 fusion.3
  72.4 0.3 copy.159
  72.7 1.0 reshape.175
  73.7 14.2 %all-to-all-done.3 = bf16[8,256,64]{1,2,0:T(8,128)(2,1)S(1)} async-done(((bf16[8,256,64]{1,2,0:T(8,128)(2,1)}), bf16[8,256,64]{1,2,0:T(8,128)(2,1)S(1)}, u32[]{:S(2)}, u32[]{:S(2)}) %all-to-all-start.3) | async-done | bytes 262176 | tf_op jit(solution)/shard_map/all_to_all | solution.py:52
  87.9 17.1 %all-to-all-start.2 = ((bf16[64,2,1024]{2,1,0:T(2,128)(2,1)}), bf16[64,2,1024]{2,1,0:T(2,128)(2,1)S(1)}, u32[]{:S(2)}, u32[]{:S(2)}) async-start(bf16[64,2,1024]{2,1,0:T(2,128)(2,1)} %reshape.175), calls=%async_computation.2 | async-start | bytes 524288 | tf_op jit(solution)/shard_map/all_to_all | solution.py:167
  105.1 0.8 reshape.177
  105.9 10.7 %all-to-all-done.2 = bf16[64,2,1024]{2,1,0:T(2,128)(2,1)S(1)} async-done(((bf16[64,2,1024]{2,1,0:T(2,128)(2,1)}), bf16[64,2,1024]{2,1,0:T(2,128)(2,1)S(1)}, u32[]{:S(2)}, u32[]{:S(2)}) %all-to-all-start.2) | async-done | bytes 262176 | tf_op jit(solution)/shard_map/all_to_all | solution.py:167
  116.6 6.4 %all-to-all-start.4 = ((f32[64,1,256]{2,1,0:T(1,128)}), f32[64,1,256]{2,1,0:T(1,128)S(1)}, u32[]{:S(2)}, u32[]{:S(2)}) async-start(f32[64,1,256]{2,1,0:T(1,128)} %reshape.177), calls=%async_computation.4 | async-start | bytes 131072 | tf_op jit(solution)/shard_map/all_to_all | solution.py:58
  123.0 0.3 reshape.176
  123.5 1.1 copy.172
  124.6 7.7 %all-to-all-done.4 = f32[64,1,256]{2,1,0:T(1,128)S(1)} async-done(((f32[64,1,256]{2,1,0:T(1,128)}), f32[64,1,256]{2,1,0:T(1,128)S(1)}, u32[]{:S(2)}, u32[]{:S(2)}) %all-to-all-start.4) | async-done | bytes 65568 | tf_op jit(solution)/shard_map/all_to_all | solution.py:58
  132.3 0.5 broadcast.102
  132.8 0.8 reduce
  133.8 0.6 copy-done.2
  134.4 0.6 multiply_subtract_fusion
  (33 shorter events, 2.6 us)
Async XLA Ops:
  0.6 59.9 %copy-start = (bf16[64,64]{1,0:T(8,128)(2,1)S(1)}, bf16[64,64]{1,0:T(8,128)(2,1)}, u32[]{:S(2)}) copy-start(bf16[64,64]{1,0:T(8,128)(2,1)} %param.13) | copy-start | bytes 24580
  2.1 21.1 %all-to-all-start.1 = ((bf16[64,2,128]{2,1,0:T(2,128)(2,1)}), bf16[64,2,128]{2,1,0:T(2,128)(2,1)S(1)}, u32[]{:S(2)}, u32[]{:S(2)}) async-start(bf16[64,2,128]{2,1,0:T(2,128)(2,1)} %reshape.173), calls=%async_computation.1 | async-start | bytes 65536 | tf_op jit(solution)/shard_map/all_to_all | solution.py:24
  14.2 1.5 %copy-start.1 = (bf16[1,64,8,256]{3,2,1,0:T(8,128)(2,1)S(1)}, bf16[1,64,8,256]{3,2,1,0:T(8,128)(2,1)}, u32[]{:S(2)}) copy-start(bf16[1,64,8,256]{3,2,1,0:T(8,128)(2,1)} %param.8) | copy-start | bytes 786436
  23.2 33.9 %all-to-all-start = ((bf16[64,2,2048]{2,1,0:T(2,128)(2,1)}), bf16[64,2,2048]{2,1,0:T(2,128)(2,1)S(1)}, u32[]{:S(2)}, u32[]{:S(2)}) async-start(bf16[64,2,2048]{2,1,0:T(2,128)(2,1)} %reshape.171), calls=%async_computation | async-start | bytes 1048576 | tf_op jit(solution)/shard_map/all_to_all | solution.py:34
  28.8 0.7 copy-start.5
  60.1 0.7 copy-start.6
  64.5 23.4 %all-to-all-start.3 = ((bf16[8,256,64]{1,2,0:T(8,128)(2,1)}), bf16[8,256,64]{1,2,0:T(8,128)(2,1)S(1)}, u32[]{:S(2)}, u32[]{:S(2)}) async-start(bf16[8,256,64]{1,2,0:T(8,128)(2,1)} %copy.170), calls=%async_computation.3 | async-start | bytes 524288 | tf_op jit(solution)/shard_map/all_to_all | solution.py:52
  87.9 28.7 %all-to-all-start.2 = ((bf16[64,2,1024]{2,1,0:T(2,128)(2,1)}), bf16[64,2,1024]{2,1,0:T(2,128)(2,1)S(1)}, u32[]{:S(2)}, u32[]{:S(2)}) async-start(bf16[64,2,1024]{2,1,0:T(2,128)(2,1)} %reshape.175), calls=%async_computation.2 | async-start | bytes 524288 | tf_op jit(solution)/shard_map/all_to_all | solution.py:167
  116.6 15.7 %all-to-all-start.4 = ((f32[64,1,256]{2,1,0:T(1,128)}), f32[64,1,256]{2,1,0:T(1,128)S(1)}, u32[]{:S(2)}, u32[]{:S(2)}) async-start(f32[64,1,256]{2,1,0:T(1,128)} %reshape.177), calls=%async_computation.4 | async-start | bytes 131072 | tf_op jit(solution)/shard_map/all_to_all | solution.py:58
  133.7 0.7 copy-start.2
  133.7 0.7 copy-start.3
  133.7 0.7 copy-start.4
where the time goes:
time: 136 us; the launch traced here: 135 us
  starting transfers between devices  47.5 us (35%)
  waiting for transfers between devices  37.8 us (28%)
  blocking collectives  25.7 us (19%)
  local copies, waits for them, and re-layouts  12.9 us (9%)
  matrix products  6.01 us (4%)
  other arithmetic  4.06 us (3%)
    all_gather x1, blocking collectives, on_device(): weight_low = lax.all_gather(group_low, 'dp', axis=0, tiled=True)  25.7 us
    all_to_all x1, starting transfers between devices, on_device(): lax.all_to_all(grad_lines, 'dom', split_axis=2, concat_axis=3, tiled=True)  17.1 us
    all_to_all x1, waiting for transfers between devices, sum_at_owner(): lax.all_to_all(tiles, axis, split_axis=0, concat_axis=0, tiled=True)  14.2 us
    all_to_all x1, starting transfers between devices, copy_for_each(): return lax.all_to_all(copies, axis, split_axis=0, concat_axis=0, tiled=True)  12.1 us
    all_to_all x1, waiting for transfers between devices, on_device(): lax.all_to_all(grad_lines, 'dom', split_axis=2, concat_axis=3, tiled=True)  10.7 us
    unnamed x25, local copies, waits for them, and re-layouts  9.8 us
    all_to_all x1, waiting for transfers between devices, summed_on_arrival(): tiles = lax.all_to_all(split_up(shard, dim, length), axis, 0, 0, tiled=True)  7.65 us
    all_to_all x1, starting transfers between devices, sum_at_owner(): lax.all_to_all(tiles, axis, split_axis=0, concat_axis=0, tiled=True)  6.44 us
  transfers between devices with their start and end apart: 5, of which 4 were waited for; matrix products, arithmetic and copies ran while one was open for 8% of the time, Pallas kernels for 0%

commit v1 on v0

--- a/solution.py
+++ b/solution.py
@@ -11,6 +11,11 @@
 beta_second = 0.95
 decay_rate = 0.1
 epsilon = 1e-08
+
+
+def gather_over(block, name, along):
+    sent = jnp.stack([block] * lax.axis_size(name))
+    return jnp.concatenate(lax.all_to_all(sent, name, 0, 0), axis=along)
 
 
 def joined_along(tiles, dim):
@@ -111,7 +116,7 @@
     keep_wide = keep_modes[:, None, None, :]
     weight_short = spectral_weight.astype(jnp.bfloat16)
     group_low = collect(weight_short, "dom", 0)
-    weight_low = lax.all_gather(group_low, "dp", axis=0, tiled=True)
+    weight_low = gather_over(group_low, "dp", 0)
     weight_low = weight_low.reshape(2, MODES, channels, channels)
     weight_real = weight_low[0]
     weight_imag = weight_low[1]

time: 136 us -> 149 us (1.096)
  waiting for transfers between devices: 37.8 us -> 61.2 us
  starting transfers between devices: 47.5 us -> 42.4 us
  blocking collectives: 25.7 us -> 21 us
    all_gather x1 -> x0, blocking collectives: 25.7 us -> none  [on_device(): weight_low = lax.all_gather(group_low, 'dp', axis=0, tiled=True)]
    all_to_all x0 -> x1, blocking collectives: none -> 21 us  [copy_for_each(): return lax.all_to_all(copies, axis, split_axis=0, concat_axis=0, tiled=True)]
    all_to_all x1, waiting for transfers between devices: 0.01 us -> 12.7 us  [in_one_piece(): lax.all_to_all(both, axis, split_axis=split_dim, concat_axis=concat_dim,...]
    all_to_all x1, waiting for transfers between devices: 5.35 us -> 14.8 us  [gather_over(): return jnp.concatenate(lax.all_to_all(sent, name, 0, 0), axis=along)]
    all_to_all x1, starting transfers between devices: 17.1 us -> 10.3 us  [on_device(): lax.all_to_all(grad_lines, 'dom', split_axis=2, concat_axis=3, tiled=True)]
    all_to_all x1, starting transfers between devices: 5.52 us -> 10.1 us  [in_one_piece(): lax.all_to_all(both, axis, split_axis=split_dim, concat_axis=concat_dim,...]
    all_to_all x1, starting transfers between devices: 6.44 us -> 3.41 us  [sum_at_owner(): lax.all_to_all(tiles, axis, split_axis=0, concat_axis=0, tiled=True)]
    all_to_all x1, waiting for transfers between devices: 14.2 us -> 16.3 us  [sum_at_owner(): lax.all_to_all(tiles, axis, split_axis=0, concat_axis=0, tiled=True)]
  transfers between devices with their start and end apart: 5 -> 5, of which waited for: 4 -> 5; matrix products, arithmetic and copies ran while one was open for 8% -> 7% of each run, Pallas kernels for 0% -> 0%
where the time goes in v1:
time: 149 us
  waiting for transfers between devices  61.2 us (41%)
  starting transfers between devices  42.4 us (28%)
  blocking collectives  21 us (14%)
  local copies, waits for them, and re-layouts  12.9 us (9%)
  matrix products  6.01 us (4%)
  other arithmetic  4.06 us (3%)
    all_to_all x1, blocking collectives, copy_for_each(): return lax.all_to_all(copies, axis, split_axis=0, concat_axis=0, tiled=True)  21 us
    all_to_all x1, waiting for transfers between devices, sum_at_owner(): lax.all_to_all(tiles, axis, split_axis=0, concat_axis=0, tiled=True)  16.3 us
    all_to_all x1, waiting for transfers between devices, gather_over(): return jnp.concatenate(lax.all_to_all(sent, name, 0, 0), axis=along)  14.8 us
    all_to_all x1, waiting for transfers between devices, in_one_piece(): lax.all_to_all(both, axis, split_axis=split_dim, concat_axis=concat_dim,...  12.7 us
    all_to_all x1, starting transfers between devices, gather_over(): return jnp.concatenate(lax.all_to_all(sent, name, 0, 0), axis=along)  12.5 us
    all_to_all x1, starting transfers between devices, on_device(): lax.all_to_all(grad_lines, 'dom', split_axis=2, concat_axis=3, tiled=True)  10.3 us
    all_to_all x1, starting transfers between devices, in_one_piece(): lax.all_to_all(both, axis, split_axis=split_dim, concat_axis=concat_dim,...  10.1 us
    all_to_all x1, waiting for transfers between devices, on_device(): lax.all_to_all(grad_lines, 'dom', split_axis=2, concat_axis=3, tiled=True)  9.82 us
  transfers between devices with their start and end apart: 5, of which 5 were waited for; matrix products, arithmetic and copies ran while one was open for 7% of the time, Pallas kernels for 0%

profile of v1, /device:TPU:2, one launch (start us, length us, event | category | flops | bytes accessed | tf_op | source)
XLA Modules:
  0.0 148.6 jit_solution(6151677100102002486)
XLA Ops:
  0.6 0.7 convert_element_type.173
  1.5 21.0 %all_to_all.53 = bf16[64,2,128]{2,1,0:T(2,128)(2,1)S(1)} all-to-all(bf16[64,2,128]{2,1,0:T(2,128)(2,1)S(1)} %reshape.170), channel_id=1, replica_groups=mesh['dp'=8,'dom'=64] {'dom'}, dimensions={0} | all-to-all | bytes 65536 | tf_op jit(solution)/shard_map/all_to_all | solution.py:29
  22.7 0.7 stack.15
  23.4 12.5 %all-to-all-start.2 = ((bf16[8,256,64]{1,2,0:T(8,128)(2,1)}), bf16[8,256,64]{1,2,0:T(8,128)(2,1)S(1)}, u32[]{:S(2)}, u32[]{:S(2)}) async-start(bf16[8,256,64]{1,2,0:T(8,128)(2,1)} %stack.15), calls=%async_computation.2 | async-start | bytes 524288 | tf_op jit(solution)/shard_map/all_to_all | solution.py:18
  35.9 0.4 copy.182
  36.3 0.5 copy-done.2
  36.9 0.4 copy.181
  37.5 1.6 %reshape.168 = bf16[64,2,2048]{2,1,0:T(2,128)(2,1)} reshape(bf16[256,2,8,64]{3,2,1,0:T(8,128)(2,1)S(1)} %fusion.144) | data formatting | bytes 1048576
  39.1 14.8 %all-to-all-done.2 = bf16[8,256,64]{1,2,0:T(8,128)(2,1)S(1)} async-done(((bf16[8,256,64]{1,2,0:T(8,128)(2,1)}), bf16[8,256,64]{1,2,0:T(8,128)(2,1)S(1)}, u32[]{:S(2)}, u32[]{:S(2)}) %all-to-all-start.2) | async-done | bytes 262176 | tf_op jit(solution)/shard_map/all_to_all | solution.py:18
  53.9 10.1 %all-to-all-start = ((bf16[64,2,2048]{2,1,0:T(2,128)(2,1)}), bf16[64,2,2048]{2,1,0:T(2,128)(2,1)S(1)}, u32[]{:S(2)}, u32[]{:S(2)}) async-start(bf16[64,2,2048]{2,1,0:T(2,128)(2,1)} %reshape.168), calls=%async_computation | async-start | bytes 1048576 | tf_op jit(solution)/shard_map/all_to_all | solution.py:39
  64.0 0.6 copy-done.6
  64.7 0.6 dynamic_slice.3
  65.3 0.6 compare_convert_fusion
  65.9 0.7 compare_select_fusion.1
  67.0 12.7 %all-to-all-done = bf16[64,2,2048]{2,1,0:T(2,128)(2,1)S(1)} async-done(((bf16[64,2,2048]{2,1,0:T(2,128)(2,1)}), bf16[64,2,2048]{2,1,0:T(2,128)(2,1)S(1)}, u32[]{:S(2)}, u32[]{:S(2)}) %all-to-all-start) | async-done | bytes 524320 | tf_op jit(solution)/shard_map/all_to_all | solution.py:39
  79.7 0.7 reshape.169
  80.6 0.3 fusion.34
  80.9 0.3 fusion.35
  81.3 0.3 copy.198
  82.1 0.3 fusion.67
  82.7 0.3 fusion.11
  83.0 0.3 copy-done.7
  83.3 0.5 fusion.47
  83.8 0.3 fusion.29
  84.1 0.3 fusion.28
  84.6 0.3 fusion.84
  84.9 0.3 fusion.77
  85.4 0.3 fusion.8
  85.7 0.3 fusion.9
  86.1 0.9 copy.217
  87.0 3.4 %all-to-all-start.4 = ((bf16[8,256,64]{1,2,0:T(8,128)(2,1)}), bf16[8,256,64]{1,2,0:T(8,128)(2,1)S(1)}, u32[]{:S(2)}, u32[]{:S(2)}) async-start(bf16[8,256,64]{1,2,0:T(8,128)(2,1)} %copy.217), calls=%async_computation.4 | async-start | bytes 524288 | tf_op jit(solution)/shard_map/all_to_all | solution.py:57
  90.9 0.4 fusion.64
  91.3 0.3 fusion.10
  91.6 0.3 fusion.3
  91.9 0.3 copy.206
  92.2 1.0 reshape.172
  93.2 16.3 %all-to-all-done.4 = bf16[8,256,64]{1,2,0:T(8,128)(2,1)S(1)} async-done(((bf16[8,256,64]{1,2,0:T(8,128)(2,1)}), bf16[8,256,64]{1,2,0:T(8,128)(2,1)S(1)}, u32[]{:S(2)}, u32[]{:S(2)}) %all-to-all-start.4) | async-done | bytes 262176 | tf_op jit(solution)/shard_map/all_to_all | solution.py:57
  109.5 10.3 %all-to-all-start.3 = ((bf16[64,2,1024]{2,1,0:T(2,128)(2,1)}), bf16[64,2,1024]{2,1,0:T(2,128)(2,1)S(1)}, u32[]{:S(2)}, u32[]{:S(2)}) async-start(bf16[64,2,1024]{2,1,0:T(2,128)(2,1)} %reshape.172), calls=%async_computation.3 | async-start | bytes 524288 | tf_op jit(solution)/shard_map/all_to_all | solution.py:172
  119.9 0.8 reshape.174
  120.6 9.8 %all-to-all-done.3 = bf16[64,2,1024]{2,1,0:T(2,128)(2,1)S(1)} async-done(((bf16[64,2,1024]{2,1,0:T(2,128)(2,1)}), bf16[64,2,1024]{2,1,0:T(2,128)(2,1)S(1)}, u32[]{:S(2)}, u32[]{:S(2)}) %all-to-all-start.3) | async-done | bytes 262176 | tf_op jit(solution)/shard_map/all_to_all | solution.py:172
  130.5 6.1 %all-to-all-start.5 = ((f32[64,1,256]{2,1,0:T(1,128)}), f32[64,1,256]{2,1,0:T(1,128)S(1)}, u32[]{:S(2)}, u32[]{:S(2)}) async-start(f32[64,1,256]{2,1,0:T(1,128)} %reshape.174), calls=%async_computation.5 | async-start | bytes 131072 | tf_op jit(solution)/shard_map/all_to_all | solution.py:63
  136.6 0.3 reshape.173
  137.1 1.1 copy.219
  138.2 7.7 %all-to-all-done.5 = f32[64,1,256]{2,1,0:T(1,128)S(1)} async-done(((f32[64,1,256]{2,1,0:T(1,128)}), f32[64,1,256]{2,1,0:T(1,128)S(1)}, u32[]{:S(2)}, u32[]{:S(2)}) %all-to-all-start.5) | async-done | bytes 65568 | tf_op jit(solution)/shard_map/all_to_all | solution.py:63
  145.9 0.5 broadcast.103
  146.4 0.8 reduce
  147.4 0.6 copy-done.3
  148.0 0.6 multiply_subtract_fusion
  (39 shorter events, 3.6 us)
Async XLA Ops:
  0.6 82.4 %copy-start = (bf16[64,64]{1,0:T(8,128)(2,1)S(1)}, bf16[64,64]{1,0:T(8,128)(2,1)}, u32[]{:S(2)}) copy-start(bf16[64,64]{1,0:T(8,128)(2,1)} %param.13) | copy-start | bytes 24580
  23.4 12.5 %copy-start.1 = (bf16[1,64,8,256]{3,2,1,0:T(8,128)(2,1)S(1)}, bf16[1,64,8,256]{3,2,1,0:T(8,128)(2,1)}, u32[]{:S(2)}) copy-start(bf16[1,64,8,256]{3,2,1,0:T(8,128)(2,1)} %param.9) | copy-start | bytes 786436
  23.4 30.5 %all-to-all-start.2 = ((bf16[8,256,64]{1,2,0:T(8,128)(2,1)}), bf16[8,256,64]{1,2,0:T(8,128)(2,1)S(1)}, u32[]{:S(2)}, u32[]{:S(2)}) async-start(bf16[8,256,64]{1,2,0:T(8,128)(2,1)} %stack.15), calls=%async_computation.2 | async-start | bytes 524288 | tf_op jit(solution)/shard_map/all_to_all | solution.py:18
  35.9 1.0 copy-start.2
  53.9 25.8 %all-to-all-start = ((bf16[64,2,2048]{2,1,0:T(2,128)(2,1)}), bf16[64,2,2048]{2,1,0:T(2,128)(2,1)S(1)}, u32[]{:S(2)}, u32[]{:S(2)}) async-start(bf16[64,2,2048]{2,1,0:T(2,128)(2,1)} %reshape.168), calls=%async_computation | async-start | bytes 1048576 | tf_op jit(solution)/shard_map/all_to_all | solution.py:39
  64.0 0.7 copy-start.6
  82.7 0.7 copy-start.7
  87.0 22.5 %all-to-all-start.4 = ((bf16[8,256,64]{1,2,0:T(8,128)(2,1)}), bf16[8,256,64]{1,2,0:T(8,128)(2,1)S(1)}, u32[]{:S(2)}, u32[]{:S(2)}) async-start(bf16[8,256,64]{1,2,0:T(8,128)(2,1)} %copy.217), calls=%async_computation.4 | async-start | bytes 524288 | tf_op jit(solution)/shard_map/all_to_all | solution.py:57
  109.5 21.0 %all-to-all-start.3 = ((bf16[64,2,1024]{2,1,0:T(2,128)(2,1)}), bf16[64,2,1024]{2,1,0:T(2,128)(2,1)S(1)}, u32[]{:S(2)}, u32[]{:S(2)}) async-start(bf16[64,2,1024]{2,1,0:T(2,128)(2,1)} %reshape.172), calls=%async_computation.3 | async-start | bytes 524288 | tf_op jit(solution)/shard_map/all_to_all | solution.py:172
  130.5 15.4 %all-to-all-start.5 = ((f32[64,1,256]{2,1,0:T(1,128)}), f32[64,1,256]{2,1,0:T(1,128)S(1)}, u32[]{:S(2)}, u32[]{:S(2)}) async-start(f32[64,1,256]{2,1,0:T(1,128)} %reshape.174), calls=%async_computation.5 | async-start | bytes 131072 | tf_op jit(solution)/shard_map/all_to_all | solution.py:63
  147.3 0.7 copy-start.3
  147.3 0.7 copy-start.4
  147.3 0.7 copy-start.5
